TPU v7x, 512 devices: a whole 4x8x8 slice. The times are simulated.
512 devices in a mesh: dp: 32 (over z, x_lo, core), tensor: 16 (over y, x_hi).
Axes of the slice: x: 4 (x_hi: 2, x_lo: 2; x = x_hi * 2 + x_lo), y: 8, z: 8, core: 2. Of those that a mesh axis runs over, the one named last changes fastest.
Arguments:
- features: bfloat16 [5120, 36864], P('tensor', 'dp'), may hold values from -24 to 24
- cotangents: bfloat16 [36864, 2048], P('dp', 'tensor'), may hold values from -24 to 24
- labels: int32 [36864], P('dp'), may hold values from 0 to 2
- diff_mask: int32 [36864], P('dp'), may hold values 0 or 1
- class_weight: float32 [3], replicated, may hold values from 0.25 to 2
- owners: int32 [16, 32], P('tensor'), may hold values from 0 to 31, each once within a row
- momentum: float32 [5120, 2048], P('dp', 'tensor'), may hold values from -3 to 3
Outputs:
- update: bfloat16 [5120, 2048], P(None, 'tensor')
- new_momentum: float32 [5120, 2048], P('dp', 'tensor')
Inputs may be any that keep to these rules, and one draw needn't show every extreme that they name: `owners`: each row names every dp index once.
All inputs are finite; a program needn't handle non-finite values. No bound on the sum of `diff_mask` on one device may be relied on, other than what follows from the above.
Results may differ from a plain program's by a relative error of at most 0.0065.
Values may be sent and summed in bfloat16 or wider, within the bound.
No kernel may reach another device: no remote copies, remote signals or barrier semaphores. Data moves between devices by JAX's collectives and lax.ppermute only.
A program may use at most 64 MiB of HBM per device.

v0:
```python
import math
import jax
import jax.numpy as jnp
from jax import lax
from jax.sharding import PartitionSpec as P

ITERS = 5
decay_rate = 0.95
quintic_first = 3.4445
quintic_second = -4.775
quintic_third = 2.0315
norm_epsilon = 1e-07


def weigh(cotangents, labels, diff_mask, class_weight, total_tokens):
    classes = jnp.arange(class_weight.shape[0], dtype=jnp.int32)
    picked = (labels[:, None] == classes[None, :]).astype(jnp.float32)
    token_weight = diff_mask.astype(jnp.float32) * jnp.sum(picked * class_weight[None, :], axis=1)
    factor = token_weight / math.sqrt(total_tokens)
    return (cotangents.astype(jnp.float32) * factor[:, None]).astype(jnp.bfloat16)


def invert(owners):
    number = owners.shape[1]
    candidates = jnp.arange(number, dtype=jnp.int32)
    matches = owners[:, None, :] == candidates[None, :, None]
    return jnp.sum(jnp.where(matches, candidates[None, None, :], 0), axis=2)


def reorder(blocks, lookup):
    return jnp.take_along_axis(blocks, jnp.transpose(lookup)[:, None, :, None], axis=0)


def orthogonalize(nesterov):
    frobenius = jnp.sqrt(jnp.sum(nesterov * nesterov, axis=(-3, -1), keepdims=True)) + norm_epsilon
    iterate = nesterov / frobenius
    for step in range(ITERS):
        gram_matrix = jnp.einsum(
            "...rhc,...rhd->...hcd", iterate, iterate, precision=lax.Precision.HIGHEST
        )
        poly_matrix = quintic_second * gram_matrix + quintic_third * jnp.einsum(
            "...hcd,...hde->...hce", gram_matrix, gram_matrix, precision=lax.Precision.HIGHEST
        )
        iterate = quintic_first * iterate + jnp.einsum(
            "...rhc,...hcd->...rhd", iterate, poly_matrix, precision=lax.Precision.HIGHEST
        )
    return iterate


def shards(features, cotangents, labels, diff_mask, class_weight, owners, momentum):
    dp_count = lax.axis_size("dp")
    tensor_count = lax.axis_size("tensor")
    local_tokens = cotangents.shape[0]
    scaled = weigh(cotangents, labels, diff_mask, class_weight, local_tokens * dp_count)
    heads_here = owners.shape[0]
    head_width = cotangents.shape[1] // heads_here
    block_rows = features.shape[0] * tensor_count // dp_count
    inverse = invert(owners)
    all_heads = lax.all_gather(scaled, "tensor", axis=1, tiled=True)
    rows_all_heads = jnp.dot(features, all_heads, preferred_element_type=jnp.float32)
    partial_grad = lax.all_to_all(
        rows_all_heads.reshape(features.shape[0], tensor_count, head_width),
        "tensor",
        split_axis=1,
        concat_axis=0,
        tiled=True,
    ).reshape(features.shape[0] * tensor_count, head_width)
    blocks = partial_grad.reshape(dp_count, block_rows, heads_here * head_width)
    in_owner_order = jnp.take(blocks, inverse[0], axis=0).reshape(
        dp_count * block_rows, heads_here * head_width
    )
    own_block = lax.psum_scatter(in_owner_order, "dp", scatter_dimension=0, tiled=True).reshape(
        block_rows, heads_here, head_width
    )
    previous = momentum.reshape(block_rows, heads_here, head_width)
    new_momentum = decay_rate * previous + own_block
    nesterov = own_block + decay_rate * new_momentum
    ortho = orthogonalize(nesterov)
    own_update = (
        (ortho * math.sqrt(block_rows))
        .astype(jnp.bfloat16)
        .reshape(block_rows, heads_here * head_width)
    )
    gathered = lax.all_gather(own_update, "dp", axis=0, tiled=True)
    placed = reorder(gathered.reshape(dp_count, block_rows, heads_here, head_width), owners)
    return (
        placed.reshape(dp_count * block_rows, heads_here * head_width),
        new_momentum.reshape(block_rows, heads_here * head_width),
    )


def solution(mesh):
    in_specs = (
        P("tensor", "dp"),
        P("dp", "tensor"),
        P("dp"),
        P("dp"),
        P(),
        P("tensor", None),
        P("dp", "tensor"),
    )
    out_specs = (P(None, "tensor"), P("dp", "tensor"))
    return jax.shard_map(shards, mesh=mesh, in_specs=in_specs, out_specs=out_specs, check_vma=False)
```

profile of v0, /device:TPU:1, one launch (start us, length us, event | category | flops | bytes accessed | tf_op | source)
XLA Modules:
  0.0 416.9 jit_solution(2855944453115864971)
XLA Ops:
  7.2 0.9 select_reduce_fusion
  8.1 0.7 multiply_multiply_fusion
  8.8 1.9 multiply_convert_fusion
  10.7 118.2 %all-gather.4.cloned.1.call-done = bf16[1152,2048]{1,0:T(8,128)(2,1)} async-done(((bf16[1152,128]{1,0:T(8,128)(2,1)}), bf16[1152,2048]{1,0:T(8,128)(2,1)}) %all-gather.4.cloned.1.call-update) | async-done | bytes 4718608 | tf_op jit(solution)/shard_map/all_gather | solution.py:59
  128.9 4.2 %convolution_bitcast_fusion = f32[40,16,8,128]{3,2,1,0:T(8,128)S(1)} fusion(bf16[320,1152]{1,0:T(8,128)(2,1)S(1)} %copy-done, bf16[1152,2048]{1,0:T(8,128)(2,1)} %all-gather.4.cloned.1.call-done), kind=kOutput, calls=%fused_computation.4 | convolution fusion | flops 1509949440 | bytes 8077312 | tf_op jit(solution)/shard_map/dot_general | solution.py:60
  133.1 1.8 copy.13
  134.9 3.9 all-to-all-start
  138.8 0.1 select_reduce_fusion.1
  139.0 0.1 broadcast_in_dim.52
  139.1 59.7 %all-to-all-done = f32[320,16,128]{2,0,1:T(8,128)S(1)} async-done(((f32[320,16,128]{2,0,1:T(8,128)}), f32[320,16,128]{2,0,1:T(8,128)S(1)}, u32[]{:S(2)}, u32[]{:S(2)}) %all-to-all-start) | async-done | bytes 2621472 | tf_op jit(solution)/shard_map/all_to_all | solution.py:61
  198.9 2.2 gather_fusion
  201.1 5.3 %bitcast_select_fusion = f32[5120,128]{1,0:T(8,128)} fusion(f32[32,160,128]{2,1,0:T(8,128)} %gather_fusion, pred[5120]{0:T(1024)(128)(4,1)S(1)} %broadcast_in_dim.52), kind=kLoop, calls=%fused_computation.3 | loop fusion | flops 655360 | bytes 5248000 | tf_op jit(solution)/shard_map/jit(_take)/select_n | solution.py:69
  206.4 121.1 %reduce-scatter.2.cloned.1.call-done = f32[160,128]{1,0:T(8,128)} async-done(((f32[5120,128]{1,0:T(8,128)}), f32[160,128]{1,0:T(8,128)}) %reduce-scatter.2.cloned.1.call-update) | async-done | bytes 81936 | tf_op jit(solution)/shard_map/reduce_scatter | solution.py:72
  327.5 1.5 multiply_reduce_fusion
  329.7 1.4 fusion.24
  331.1 0.2 fusion.10
  331.3 1.2 fusion
  332.5 0.4 fusion.22
  332.9 0.2 fusion.9
  333.1 0.2 fusion.1
  333.4 0.4 fusion.19
  333.8 0.2 fusion.8
  334.0 0.2 fusion.2
  334.2 0.4 fusion.16
  334.7 0.2 fusion.7
  334.9 0.2 fusion.3
  335.1 0.4 fusion.13
  335.6 0.2 fusion.6
  335.8 0.8 fusion.11
  336.9 68.0 %all-gather.6.cloned.1.call-done = bf16[5120,1,128]{2,0,1:T(8,128)(2,1)} async-done(((bf16[160,1,128]{2,0,1:T(8,128)(2,1)}), bf16[5120,1,128]{2,0,1:T(8,128)(2,1)}) %all-gather.6.cloned.1.call-update) | async-done | bytes 1310736 | tf_op jit(solution)/shard_map/all_gather | solution.py:84
  404.9 2.1 gather_fusion.1
  407.0 3.4 bitcast_select_fusion.1
  (23 shorter events, 0.5 us)
Async XLA Ops:
  7.2 121.8 %copy-start = (bf16[320,1152]{1,0:T(8,128)(2,1)S(1)}, bf16[320,1152]{1,0:T(8,128)(2,1)}, u32[]{:S(2)}) copy-start(bf16[320,1152]{1,0:T(8,128)(2,1)} %param.7) | copy-start | bytes 2211844
  7.2 121.7 %all-gather.4.cloned.1.call-start = ((), (), s32[]{:S(2)}) async-start(), calls=%async_computation.2 | async-start | bytes 5013504 | tf_op jit(solution)/shard_map/all_gather | solution.py:59
  134.9 3.9 copy-start.3
  134.9 64.0 %all-to-all-start = ((f32[320,16,128]{2,0,1:T(8,128)}), f32[320,16,128]{2,0,1:T(8,128)S(1)}, u32[]{:S(2)}, u32[]{:S(2)}) async-start(f32[320,16,128]{2,0,1:T(8,128)} %bitcast.100), calls=%async_computation | async-start | bytes 5242880 | tf_op jit(solution)/shard_map/all_to_all | solution.py:61
  138.8 188.7 %reduce-scatter.2.cloned.1.call-start = ((), (), s32[]{:S(2)}) async-start(), calls=%async_computation.3 | async-start | bytes 2703360 | tf_op jit(solution)/shard_map/reduce_scatter | solution.py:72
  206.3 121.1 %copy-start.1 = (f32[160,128]{1,0:T(8,128)S(1)}, f32[160,128]{1,0:T(8,128)}, u32[]{:S(2)}) copy-start(f32[160,128]{1,0:T(8,128)} %param.13) | copy-start | bytes 245764
  206.4 198.6 %all-gather.6.cloned.1.call-start = ((), (), s32[]{:S(2)}) async-start(), calls=%async_computation.4 | async-start | bytes 1351680 | tf_op jit(solution)/shard_map/all_gather | solution.py:84
  329.0 78.1 %copy-start.2 = (f32[160,128]{1,0:T(8,128)}, f32[160,128]{1,0:T(8,128)S(1)}, u32[]{:S(2)}) copy-start(f32[160,128]{1,0:T(8,128)S(1)} %get-tuple-element.3) | copy-start | bytes 245764
Sparse Core Ops, SparseCore 0:
  11.6 117.2 all-gather.3
  206.5 120.9 reduce-scatter.1
  336.8 68.0 all-gather.5
where the time goes:
time: 417 us
  waiting for transfers between devices  367 us (88%)
  between operations  14.6 us (4%)
  other arithmetic  13.8 us (3%)
  matrix products  11 us (3%)
  local copies, waits for them, and re-layouts  6.46 us (2%)
    reduce_scatter x1, waiting for transfers between devices, shards(): lax.psum_scatter(in_owner_order, 'dp', scatter_dimension=0, tiled=True)  121 us
    all_gather x1, waiting for transfers between devices, shards(): all_heads = lax.all_gather(scaled, 'tensor', axis=1, tiled=True)  118 us
    all_gather x1, waiting for transfers between devices, shards(): gathered = lax.all_gather(own_update, 'dp', axis=0, tiled=True)  68 us
    all_to_all x1, waiting for transfers between devices, shards(): lax.all_to_all(rows_all_heads.reshape(features.shape[0], tensor_count, he...  59.7 us
  transfers between devices with their start and end apart: 4, of which 4 were waited for; matrix products, arithmetic and copies ran while one was open for 0% of the time, Pallas kernels for 0%

commit v1 on v0

--- a/solution.py
+++ b/solution.py
@@ -58,12 +58,20 @@
     inverse = invert(owners)
     all_heads = lax.all_gather(scaled, "tensor", axis=1, tiled=True)
     rows_all_heads = jnp.dot(features, all_heads, preferred_element_type=jnp.float32)
-    partial_grad = lax.all_to_all(
-        rows_all_heads.reshape(features.shape[0], tensor_count, head_width),
-        "tensor",
-        split_axis=1,
-        concat_axis=0,
-        tiled=True,
+    partial_grad = jnp.concatenate(
+        lax.all_to_all(
+            jnp.stack(
+                jnp.split(
+                    rows_all_heads.reshape(features.shape[0], tensor_count, head_width),
+                    lax.axis_size("tensor"),
+                    axis=1,
+                )
+            ),
+            "tensor",
+            0,
+            0,
+        ),
+        axis=0,
     ).reshape(features.shape[0] * tensor_count, head_width)
     blocks = partial_grad.reshape(dp_count, block_rows, heads_here * head_width)
     in_owner_order = jnp.take(blocks, inverse[0], axis=0).reshape(

time: 417 us -> 429 us (1.029)
  local copies, waits for them, and re-layouts: 6.46 us -> 18.3 us
    unnamed x8 -> x24, local copies, waits for them, and re-layouts: 0.02 us -> 10.6 us
where the time goes in v1:
time: 429 us
  waiting for transfers between devices  367 us (86%)
  local copies, waits for them, and re-layouts  18.3 us (4%)
  between operations  14.7 us (3%)
  other arithmetic  13.8 us (3%)
  matrix products  11 us (3%)
    reduce_scatter x1, waiting for transfers between devices, shards(): lax.psum_scatter(in_owner_order, 'dp', scatter_dimension=0, tiled=True)  121 us
    all_gather x1, waiting for transfers between devices, shards(): all_heads = lax.all_gather(scaled, 'tensor', axis=1, tiled=True)  118 us
    all_gather x1, waiting for transfers between devices, shards(): gathered = lax.all_gather(own_update, 'dp', axis=0, tiled=True)  68.1 us
    all_to_all x1, waiting for transfers between devices, shards(): lax.all_to_all(jnp.stack(jnp.split(rows_all_heads.reshape(features.shape[...  59.7 us
    unnamed x24, local copies, waits for them, and re-layouts  10.6 us
  transfers between devices with their start and end apart: 4, of which 4 were waited for; matrix products, arithmetic and copies ran while one was open for 0% of the time, Pallas kernels for 0%

profile of v1, /device:TPU:1, one launch (start us, length us, event | category | flops | bytes accessed | tf_op | source)
XLA Modules:
  0.0 428.8 jit_solution(1184954164391256121)
XLA Ops:
  7.2 0.9 select_reduce_fusion
  8.1 0.7 multiply_multiply_fusion
  8.8 1.9 multiply_convert_fusion
  10.7 118.2 %all-gather.4.cloned.1.call-done = bf16[1152,2048]{1,0:T(8,128)(2,1)} async-done(((bf16[1152,128]{1,0:T(8,128)(2,1)}), bf16[1152,2048]{1,0:T(8,128)(2,1)}) %all-gather.4.cloned.1.call-update) | async-done | bytes 4718608 | tf_op jit(solution)/shard_map/all_gather | solution.py:59
  128.9 4.2 convolution_bitcast_fusion
  133.6 2.3 fusion.27
  136.0 0.7 constant_dynamic-update-slice_fusion.15
  136.6 0.7 constant_dynamic-update-slice_fusion.14
  137.3 0.7 constant_dynamic-update-slice_fusion.13
  138.0 0.7 constant_dynamic-update-slice_fusion.12
  138.6 0.7 constant_dynamic-update-slice_fusion.11
  139.3 0.7 constant_dynamic-update-slice_fusion.10
  140.0 0.7 constant_dynamic-update-slice_fusion.9
  141.3 0.7 constant_dynamic-update-slice_fusion.7
  142.0 0.7 constant_dynamic-update-slice_fusion.6
  142.7 0.7 constant_dynamic-update-slice_fusion.5
  143.4 0.7 constant_dynamic-update-slice_fusion.4
  144.0 0.7 constant_dynamic-update-slice_fusion.3
  144.7 0.7 constant_dynamic-update-slice_fusion.2
  145.4 0.7 constant_dynamic-update-slice_fusion.1
  146.7 3.9 all-to-all-start
  151.0 59.7 %all-to-all-done = f32[16,320,1,128]{3,1,2,0:T(8,128)S(1)} async-done(((f32[16,320,1,128]{3,1,2,0:T(8,128)}), f32[16,320,1,128]{3,1,2,0:T(8,128)S(1)}, u32[]{:S(2)}, u32[]{:S(2)}) %all-to-all-start) | async-done | bytes 2621472 | tf_op jit(solution)/shard_map/all_to_all | solution.py:62
  210.7 2.2 gather_fusion
  212.9 5.3 %bitcast_select_fusion = f32[5120,128]{1,0:T(8,128)} fusion(f32[32,160,128]{2,1,0:T(8,128)} %gather_fusion, pred[5120]{0:T(1024)(128)(4,1)S(1)} %broadcast_in_dim.52), kind=kLoop, calls=%fused_computation.2 | loop fusion | flops 655360 | bytes 5248000 | tf_op jit(solution)/shard_map/jit(_take)/select_n | solution.py:77
  218.3 121.1 %reduce-scatter.2.cloned.1.call-done = f32[160,128]{1,0:T(8,128)} async-done(((f32[5120,128]{1,0:T(8,128)}), f32[160,128]{1,0:T(8,128)}) %reduce-scatter.2.cloned.1.call-update) | async-done | bytes 81936 | tf_op jit(solution)/shard_map/reduce_scatter | solution.py:80
  339.3 1.5 multiply_reduce_fusion
  341.5 1.4 fusion.24
  343.2 1.2 fusion
  347.6 0.8 fusion.11
  348.7 68.1 %all-gather.6.cloned.1.call-done = bf16[5120,1,128]{2,0,1:T(8,128)(2,1)} async-done(((bf16[160,1,128]{2,0,1:T(8,128)(2,1)}), bf16[5120,1,128]{2,0,1:T(8,128)(2,1)}) %all-gather.6.cloned.1.call-update) | async-done | bytes 1310736 | tf_op jit(solution)/shard_map/all_gather | solution.py:92
  416.8 2.1 gather_fusion.1
  418.9 3.4 bitcast_select_fusion.1
  (40 shorter events, 6.0 us)
Async XLA Ops:
  7.2 121.8 %copy-start = (bf16[320,1152]{1,0:T(8,128)(2,1)S(1)}, bf16[320,1152]{1,0:T(8,128)(2,1)}, u32[]{:S(2)}) copy-start(bf16[320,1152]{1,0:T(8,128)(2,1)} %param.7) | copy-start | bytes 2211844
  7.2 121.7 %all-gather.4.cloned.1.call-start = ((), (), s32[]{:S(2)}) async-start(), calls=%async_computation.2 | async-start | bytes 5013504 | tf_op jit(solution)/shard_map/all_gather | solution.py:59
  146.7 3.9 copy-start.3
  146.7 64.0 %all-to-all-start = ((f32[16,320,1,128]{3,1,2,0:T(8,128)}), f32[16,320,1,128]{3,1,2,0:T(8,128)S(1)}, u32[]{:S(2)}, u32[]{:S(2)}) async-start(f32[16,320,1,128]{3,1,2,0:T(8,128)} %constant_dynamic-update-slice_fusion), calls=%async_computation | async-start | bytes 5242880 | tf_op jit(solution)/shard_map/all_to_all | solution.py:62
  150.6 188.7 %reduce-scatter.2.cloned.1.call-start = ((), (), s32[]{:S(2)}) async-start(), calls=%async_computation.3 | async-start | bytes 2703360 | tf_op jit(solution)/shard_map/reduce_scatter | solution.py:80
  218.2 121.1 %copy-start.1 = (f32[160,128]{1,0:T(8,128)S(1)}, f32[160,128]{1,0:T(8,128)}, u32[]{:S(2)}) copy-start(f32[160,128]{1,0:T(8,128)} %param.13) | copy-start | bytes 245764
  218.2 198.6 %all-gather.6.cloned.1.call-start = ((), (), s32[]{:S(2)}) async-start(), calls=%async_computation.4 | async-start | bytes 1351680 | tf_op jit(solution)/shard_map/all_gather | solution.py:92
  340.8 78.1 %copy-start.2 = (f32[160,128]{1,0:T(8,128)}, f32[160,128]{1,0:T(8,128)S(1)}, u32[]{:S(2)}) copy-start(f32[160,128]{1,0:T(8,128)S(1)} %get-tuple-element.3) | copy-start | bytes 245764
Sparse Core Ops, SparseCore 0:
  11.6 117.2 all-gather.3
  218.3 120.9 reduce-scatter.1
  348.6 68.1 all-gather.5

commit v2 on v0

--- a/solution.py
+++ b/solution.py
@@ -81,7 +81,9 @@
         .astype(jnp.bfloat16)
         .reshape(block_rows, heads_here * head_width)
     )
-    gathered = lax.all_gather(own_update, "dp", axis=0, tiled=True)
+    gathered = jnp.concatenate(
+        lax.all_to_all(jnp.stack([own_update] * lax.axis_size("dp")), "dp", 0, 0), axis=0
+    )
     placed = reorder(gathered.reshape(dp_count, block_rows, heads_here, head_width), owners)
     return (
         placed.reshape(dp_count * block_rows, heads_here * head_width),

time: 417 us -> 391 us (0.938)
  waiting for transfers between devices: 367 us -> 333 us
  starting transfers between devices: 3.98 us -> 12.2 us
    all_gather x1 -> x0, waiting for transfers between devices: 68 us -> none  [shards(): gathered = lax.all_gather(own_update, 'dp', axis=0, tiled=True)]
    all_to_all x0 -> x1, waiting for transfers between devices: none -> 33.5 us  [shards(): lax.all_to_all(jnp.stack([own_update] * lax.axis_size('dp')), 'dp', 0, 0)]
    all_to_all x0 -> x1, starting transfers between devices: none -> 8.23 us  [shards(): lax.all_to_all(jnp.stack([own_update] * lax.axis_size('dp')), 'dp', 0, 0)]
where the time goes in v2:
time: 391 us; the launch traced here: 390 us
  waiting for transfers between devices  333 us (85%)
  between operations  14.9 us (4%)
  other arithmetic  13.8 us (4%)
  starting transfers between devices  12.2 us (3%)
  matrix products  10.4 us (3%)
  local copies, waits for them, and re-layouts  6.39 us (2%)
    reduce_scatter x1, waiting for transfers between devices, shards(): lax.psum_scatter(in_owner_order, 'dp', scatter_dimension=0, tiled=True)  121 us
    all_gather x1, waiting for transfers between devices, shards(): all_heads = lax.all_gather(scaled, 'tensor', axis=1, tiled=True)  118 us
    all_to_all x1, waiting for transfers between devices, shards(): lax.all_to_all(rows_all_heads.reshape(features.shape[0], tensor_count, he...  59.7 us
    all_to_all x1, waiting for transfers between devices, shards(): lax.all_to_all(jnp.stack([own_update] * lax.axis_size('dp')), 'dp', 0, 0)  33.5 us
    all_to_all x1, starting transfers between devices, shards(): lax.all_to_all(jnp.stack([own_update] * lax.axis_size('dp')), 'dp', 0, 0)  8.23 us
  transfers between devices with their start and end apart: 4, of which 4 were waited for; matrix products, arithmetic and copies ran while one was open for 0% of the time, Pallas kernels for 0%

profile of v2, /device:TPU:1, one launch (start us, length us, event | category | flops | bytes accessed | tf_op | source)
XLA Modules:
  0.0 390.2 jit_solution(3088976849691366537)
XLA Ops:
  7.2 0.9 select_reduce_fusion
  8.1 0.7 multiply_multiply_fusion
  8.8 1.9 multiply_convert_fusion
  10.7 118.2 %all-gather.2.cloned.1.call-done = bf16[1152,2048]{1,0:T(8,128)(2,1)} async-done(((bf16[1152,128]{1,0:T(8,128)(2,1)}), bf16[1152,2048]{1,0:T(8,128)(2,1)}) %all-gather.2.cloned.1.call-update) | async-done | bytes 4718608 | tf_op jit(solution)/shard_map/all_gather | solution.py:59
  128.9 4.2 %convolution_bitcast_fusion = f32[40,16,8,128]{3,2,1,0:T(8,128)S(1)} fusion(bf16[320,1152]{1,0:T(8,128)(2,1)S(1)} %copy-done, bf16[1152,2048]{1,0:T(8,128)(2,1)} %all-gather.2.cloned.1.call-done), kind=kOutput, calls=%fused_computation.4 | convolution fusion | flops 1509949440 | bytes 8077312 | tf_op jit(solution)/shard_map/dot_general | solution.py:60
  133.1 1.8 copy.13
  134.9 3.9 all-to-all-start
  139.2 59.7 %all-to-all-done = f32[320,16,128]{2,0,1:T(8,128)S(1)} async-done(((f32[320,16,128]{2,0,1:T(8,128)}), f32[320,16,128]{2,0,1:T(8,128)S(1)}, u32[]{:S(2)}, u32[]{:S(2)}) %all-to-all-start) | async-done | bytes 2621472 | tf_op jit(solution)/shard_map/all_to_all | solution.py:61
  198.9 2.2 gather_fusion
  201.1 5.3 %bitcast_select_fusion = f32[5120,128]{1,0:T(8,128)} fusion(f32[32,160,128]{2,1,0:T(8,128)} %gather_fusion, pred[5120]{0:T(1024)(128)(4,1)S(1)} %broadcast_in_dim.52), kind=kLoop, calls=%fused_computation.3 | loop fusion | flops 655360 | bytes 5248000 | tf_op jit(solution)/shard_map/jit(_take)/select_n | solution.py:69
  206.4 121.1 %reduce-scatter.2.cloned.1.call-done = f32[160,128]{1,0:T(8,128)} async-done(((f32[5120,128]{1,0:T(8,128)}), f32[160,128]{1,0:T(8,128)}) %reduce-scatter.2.cloned.1.call-update) | async-done | bytes 81936 | tf_op jit(solution)/shard_map/reduce_scatter | solution.py:72
  327.5 1.5 multiply_reduce_fusion
  329.7 1.4 fusion.25
  331.1 0.2 fusion.10
  331.3 1.2 fusion
  332.5 0.4 fusion.23
  333.0 0.2 fusion.9
  333.2 0.2 fusion.1
  333.4 0.4 fusion.20
  333.8 0.2 fusion.8
  334.0 0.2 fusion.2
  334.3 0.4 fusion.17
  334.7 0.2 fusion.7
  334.9 0.2 fusion.3
  335.1 0.4 fusion.14
  335.6 0.2 fusion.6
  335.8 0.2 fusion.12
  336.0 1.2 stack.3
  337.3 8.2 %all-to-all-start.1 = ((bf16[32,160,128]{2,1,0:T(8,128)(2,1)}), bf16[32,160,128]{2,1,0:T(8,128)(2,1)S(1)}, u32[]{:S(2)}, u32[]{:S(2)}) async-start(bf16[32,160,128]{2,1,0:T(8,128)(2,1)} %stack.3), calls=%async_computation.2 | async-start | bytes 2621440 | tf_op jit(solution)/shard_map/all_to_all | solution.py:85
  345.7 33.5 %all-to-all-done.1 = bf16[32,160,128]{2,1,0:T(8,128)(2,1)S(1)} async-done(((bf16[32,160,128]{2,1,0:T(8,128)(2,1)}), bf16[32,160,128]{2,1,0:T(8,128)(2,1)S(1)}, u32[]{:S(2)}, u32[]{:S(2)}) %all-to-all-start.1) | async-done | bytes 1310752 | tf_op jit(solution)/shard_map/all_to_all | solution.py:85
  379.2 0.8 gather_fusion.1
  380.0 3.4 bitcast_select_fusion.1
  (23 shorter events, 0.6 us)
Async XLA Ops:
  7.2 121.8 %copy-start = (bf16[320,1152]{1,0:T(8,128)(2,1)S(1)}, bf16[320,1152]{1,0:T(8,128)(2,1)}, u32[]{:S(2)}) copy-start(bf16[320,1152]{1,0:T(8,128)(2,1)} %param.7) | copy-start | bytes 2211844
  7.2 121.7 %all-gather.2.cloned.1.call-start = ((), (), s32[]{:S(2)}) async-start(), calls=%async_computation.3 | async-start | bytes 5013504 | tf_op jit(solution)/shard_map/all_gather | solution.py:59
  134.9 3.9 %copy-start.3 = (s32[1,32]{1,0:T(1,128)S(1)}, s32[1,32]{1,0:T(1,128)}, u32[]{:S(2)}) copy-start(s32[1,32]{1,0:T(1,128)} %param.12) | copy-start | bytes 388
  134.9 64.0 %all-to-all-start = ((f32[320,16,128]{2,0,1:T(8,128)}), f32[320,16,128]{2,0,1:T(8,128)S(1)}, u32[]{:S(2)}, u32[]{:S(2)}) async-start(f32[320,16,128]{2,0,1:T(8,128)} %bitcast.103), calls=%async_computation | async-start | bytes 5242880 | tf_op jit(solution)/shard_map/all_to_all | solution.py:61
  138.8 188.7 %reduce-scatter.2.cloned.1.call-start = ((), (), s32[]{:S(2)}) async-start(), calls=%async_computation.4 | async-start | bytes 2703360 | tf_op jit(solution)/shard_map/reduce_scatter | solution.py:72
  206.3 121.1 %copy-start.1 = (f32[160,128]{1,0:T(8,128)S(1)}, f32[160,128]{1,0:T(8,128)}, u32[]{:S(2)}) copy-start(f32[160,128]{1,0:T(8,128)} %param.13) | copy-start | bytes 245764
  329.0 8.3 %copy-start.2 = (f32[160,128]{1,0:T(8,128)}, f32[160,128]{1,0:T(8,128)S(1)}, u32[]{:S(2)}) copy-start(f32[160,128]{1,0:T(8,128)S(1)} %get-tuple-element.3) | copy-start | bytes 245764
  337.3 41.9 %all-to-all-start.1 = ((bf16[32,160,128]{2,1,0:T(8,128)(2,1)}), bf16[32,160,128]{2,1,0:T(8,128)(2,1)S(1)}, u32[]{:S(2)}, u32[]{:S(2)}) async-start(bf16[32,160,128]{2,1,0:T(8,128)(2,1)} %stack.3), calls=%async_computation.2 | async-start | bytes 2621440 | tf_op jit(solution)/shard_map/all_to_all | solution.py:85
Sparse Core Ops, SparseCore 0:
  11.6 117.2 all-gather.1
  206.5 120.9 reduce-scatter.1
